TPU v7x, 256 devices: a whole 4x4x8 slice. The times are simulated.
256 devices in a mesh: dp: 32 (over x, z_lo, core), fsdp: 8 (over y, z_hi).
Axes of the slice: x: 4, y: 4, z: 8 (z_hi: 2, z_lo: 4; z = z_hi * 4 + z_lo), core: 2. Of those that a mesh axis runs over, the one named last changes fastest.
Arguments:
- stream_rows: bfloat16 [16384, 4096], P(('dp', 'fsdp')), may hold values from -6 to 6
- ln_gain: float32 [4096], replicated, may hold values from 0.1 to 1.9
- ln_bias: float32 [4096], replicated, may hold values from -2 to 2
- w_q: bfloat16 [4096, 2048], P(None, 'fsdp')
- w_k: bfloat16 [4096, 2048], P(None, 'fsdp')
- w_v: bfloat16 [4096, 2048], P(None, 'fsdp'), may hold values from -0.09375 to 0.09375
- w_o: bfloat16 [2048, 4096], P('fsdp'), may hold values from -0.1875 to 0.1875
- scale_ls: float32 [4096], P('fsdp'), may hold values from 0.5 to 2
- sides: int32 [32, 1], P('dp'), may hold values from 10 to 18, as said below
- offsets: int32 [32, 1], P('dp'), may hold values from 0 to 0, as said below
- owners: int32 [32, 1], replicated, may hold values from 0 to 31, as said below
Outputs:
- delivered: bfloat16 [32, 1, 81, 4, 4096], P('dp', None, None, None, 'fsdp')
Inputs may be any that keep to these rules, and one draw needn't show every extreme that they name: `sides`: every side is even, and some image has side 18 in every draw. `offsets`: within a group the images lie back to back in index order from row 0, each taking 5 + side * side rows; the rows after the last image are padding. owners[g, j] = (g + c_j) mod 32, with offsets c_j that differ between image indices j; so the images of one group have different owners and every owner receives exactly one image of each index j.
All inputs are finite; a program needn't handle non-finite values.
Results may differ from a plain program's by a relative error of at most 0.012.
Values may be sent and summed in bfloat16 or wider, within the bound.
No kernel may reach another device: no remote copies, remote signals or barrier semaphores. Data moves between devices by JAX's collectives and lax.ppermute only.
A program may use at most 128 MiB of HBM per device.

v0:
```python
import math
import jax
import jax.numpy as jnp
from jax import lax
from jax.sharding import PartitionSpec as P

HEAD = 128
EXTRA = 5
CAP = 81
norm_eps = 1e-06


def shifted(array, axis, by):
    count = lax.axis_size(axis)
    return lax.ppermute(array, axis, [(i, (i + by) % count) for i in range(count)])


def layer_norm(raw_rows, ln_gain, ln_bias):
    values = raw_rows.astype(jnp.float32)
    centre = jnp.mean(values, axis=-1, keepdims=True)
    spread = jnp.mean(jnp.square(values - centre), axis=-1, keepdims=True)
    return ((values - centre) * lax.rsqrt(spread + norm_eps) * ln_gain + ln_bias).astype(
        jnp.bfloat16
    )


def row_layout(side_row, offset_row, count):
    row_ids = jnp.arange(count, dtype=jnp.int32)
    lengths = EXTRA + side_row * side_row
    inside = (
        (row_ids[:, None] >= offset_row[None, :])
        & (row_ids[:, None] < (offset_row + lengths)[None, :])
    ).astype(jnp.int32)
    covered = jnp.sum(inside, axis=1)
    image_ids = jnp.arange(side_row.shape[0], dtype=jnp.int32)
    segment = jnp.sum(inside * image_ids[None, :], axis=1) + (1 - covered) * side_row.shape[0]
    first_row = jnp.sum(inside * offset_row[None, :], axis=1)
    side_len = jnp.sum(inside * side_row[None, :], axis=1) + (1 - covered)
    patch_id = row_ids - first_row - EXTRA
    is_patch = (covered == 1) & (patch_id >= 0)
    clipped = jnp.maximum(patch_id, 0)
    across = clipped // side_len
    along = clipped % side_len
    side_float = side_len.astype(jnp.float32)
    coord_one = jnp.where(
        is_patch,
        (2 * across + 1).astype(jnp.float32) / side_float - 1.0,
        jnp.zeros_like(side_float),
    )
    coord_two = jnp.where(
        is_patch, (2 * along + 1).astype(jnp.float32) / side_float - 1.0, jnp.zeros_like(side_float)
    )
    return (segment, coord_one, coord_two)


def rotary_tables(coord_one, coord_two, head_size):
    dims = jnp.arange(head_size, dtype=jnp.int32)
    first_half = dims < head_size // 2
    freq_index = (dims % (head_size // 4)).astype(jnp.float32)
    rates = 3.0 * jnp.power(jnp.ones_like(freq_index) * 1.2, freq_index)
    coords = jnp.where(first_half[None, :], coord_one[:, None], coord_two[:, None])
    angles = coords * rates[None, :]
    return (jnp.cos(angles), jnp.sin(angles))


def rotate(tensor, cosine, sine_tab):
    row_count, head_count, head_size = tensor.shape
    quarters = tensor.reshape(row_count, head_count, 2, 2, head_size // 4)
    turned = jnp.stack([-quarters[:, :, :, 1], quarters[:, :, :, 0]], axis=3).reshape(tensor.shape)
    return tensor * cosine[:, None, :] + turned * sine_tab[:, None, :]


def softmax_rounded(scores):
    top = jnp.max(scores, axis=-1, keepdims=True)
    expo = jnp.exp(scores - top)
    return (expo / jnp.sum(expo, axis=-1, keepdims=True)).astype(jnp.bfloat16)


def merge_image(rows_all, side_len, offset):
    slot = jnp.arange(CAP, dtype=jnp.int32)
    half_side = side_len // 2
    across = slot // half_side
    along = slot % half_side
    valid = slot < half_side * half_side
    corner = jnp.arange(4, dtype=jnp.int32)
    source_rows = (
        offset
        + EXTRA
        + (2 * across[:, None] + corner[None, :] // 2) * side_len
        + 2 * along[:, None]
        + corner[None, :] % 2
    )
    source_rows = jnp.where(valid[:, None], source_rows, jnp.zeros_like(source_rows))
    picked = jnp.take(rows_all, source_rows, axis=0)
    return jnp.where(valid[:, None, None], picked, jnp.zeros_like(picked))


def dense_attention(queries, key_rows, value_rows, segment):
    group_rows = queries.shape[0]
    block_rows = 512

    def one_block(block_id):
        scores = jnp.einsum(
            "qhd,khd->hqk", queries, key_rows, preferred_element_type=jnp.float32
        ) / math.sqrt(HEAD)
        allowed = segment[None, :, None] == segment[None, None, :]
        scores = jnp.where(allowed, scores, jnp.full_like(scores, -1e30))
        weights = softmax_rounded(scores)
        return jnp.einsum(
            "hqk,khd->qhd", weights, value_rows, preferred_element_type=jnp.float32
        ).astype(jnp.bfloat16)

    stacked = lax.map(one_block, jnp.arange(group_rows // block_rows, dtype=jnp.int32))
    return stacked.reshape(queries.shape)


def body(stream_rows, ln_gain, ln_bias, w_q, w_k, w_v, w_o, scale_ls, sides, offsets, owners):
    fsdp_count = lax.axis_size("fsdp")
    group_rows = stream_rows.shape[0] * fsdp_count
    head_cols = w_q.shape[1]
    local_heads = head_cols // HEAD
    side_row = sides[0]
    offset_row = offsets[0]
    shard_rows = lax.all_gather(
        layer_norm(stream_rows, ln_gain, ln_bias), "fsdp", axis=0, tiled=True
    )
    projected = jnp.concatenate(
        [
            jnp.dot(shard_rows, w_q, preferred_element_type=jnp.float32),
            jnp.dot(shard_rows, w_k, preferred_element_type=jnp.float32),
            jnp.dot(shard_rows, w_v, preferred_element_type=jnp.float32),
        ],
        axis=1,
    )
    residual = lax.all_to_all(stream_rows, "fsdp", split_axis=1, concat_axis=0, tiled=True)
    segment, coord_one, coord_two = row_layout(side_row, offset_row, group_rows)
    cosine, sine_tab = rotary_tables(coord_one, coord_two, HEAD)
    queries = rotate(
        projected[:, :head_cols].reshape(group_rows, local_heads, HEAD), cosine, sine_tab
    ).astype(jnp.bfloat16)
    key_rows = rotate(
        projected[:, head_cols : 2 * head_cols].reshape(group_rows, local_heads, HEAD),
        cosine,
        sine_tab,
    ).astype(jnp.bfloat16)
    value_rows = (
        projected[:, 2 * head_cols :].astype(jnp.bfloat16).reshape(group_rows, local_heads, HEAD)
    )
    attended = dense_attention(queries, key_rows, value_rows, segment)
    partial_sum = jnp.dot(
        attended.reshape(group_rows, head_cols), w_o, preferred_element_type=jnp.float32
    )
    branch = lax.psum_scatter(
        partial_sum.astype(jnp.bfloat16), "fsdp", scatter_dimension=1, tiled=True
    ).astype(jnp.float32)
    updated = (residual.astype(jnp.float32) + scale_ls * branch).astype(jnp.bfloat16)

    def merge_entry(image_info):
        return merge_image(updated, image_info[0], image_info[1])

    merged = lax.map(merge_entry, (side_row, offset_row))
    group_id = lax.axis_index("dp")
    group_count = lax.axis_size("dp")
    targets = lax.dynamic_index_in_dim(owners, group_id, 0, keepdims=False)
    distance = (targets - group_id + group_count) % group_count
    carried = merged
    for level in range((group_count - 1).bit_length()):
        moved = shifted(carried, "dp", 1 << level)
        taken = distance // (1 << level) % 2 == 1
        carried = jnp.where(taken[:, None, None, None], moved, carried)
    return carried[None]


def solution(mesh):
    return jax.shard_map(
        body,
        mesh=mesh,
        in_specs=(
            P(("dp", "fsdp"), None),
            P(),
            P(),
            P(None, "fsdp"),
            P(None, "fsdp"),
            P(None, "fsdp"),
            P("fsdp", None),
            P("fsdp"),
            P("dp", None),
            P("dp", None),
            P(),
        ),
        out_specs=P("dp", None, None, None, "fsdp"),
        check_vma=False,
    )
```

profile of v0, /device:TPU:8, one launch (start us, length us, event | category | flops | bytes accessed | tf_op | source)
XLA Modules:
  0.0 330.2 jit_solution(13146252154444454191)
XLA Ops:
  6.5 0.0 copy-start
  6.5 0.0 all-gather.2.cloned.1.call-start
  6.5 1.4 convert_reduce_fusion
  7.9 1.3 fusion.4
  9.3 2.1 fusion.7
  11.4 0.0 all-gather.2.cloned.1.call-update
  11.4 0.0 reduce-scatter.2.cloned.1.call-start
  12.8 0.1 add_select_fusion.2
  13.0 0.2 broadcast_compare_fusion
  13.2 1.0 fusion.17
  14.2 106.2 %all-gather.2.cloned.1.call-done = bf16[512,4096]{1,0:T(8,128)(2,1)} async-done(((bf16[64,4096]{1,0:T(8,128)(2,1)}), bf16[512,4096]{1,0:T(8,128)(2,1)}) %all-gather.2.cloned.1.call-update) | async-done | bytes 4194320 | tf_op jit(solution)/shard_map/all_gather | solution.py:124
  120.4 0.0 copy-start.3
  120.4 0.0 copy-start.4
  120.4 4.3 %fusion.47 = f32[512,256]{0,1:T(8,128)S(1)} fusion(bf16[512,4096]{1,0:T(8,128)(2,1)} %all-gather.2.cloned.1.call-done, bf16[4096,256]{1,0:T(8,128)(2,1)} %param.14), kind=kOutput, calls=%fused_computation.99 | convolution fusion | flops 1073741824 | bytes 6815744 | tf_op jit(solution)/shard_map/dot_general | solution.py:129
  124.7 0.0 copy-done.3
  124.7 0.4 copy-done.4
  125.1 1.3 fusion.48
  126.5 0.1 pad_maximum_fusion
  126.6 0.3 fusion.13
  126.9 1.0 fusion.46
  127.9 4.2 %convolution_convert_fusion.2 = bf16[512,256]{0,1:T(8,128)(2,1)S(1)} fusion(bf16[512,4096]{1,0:T(8,128)(2,1)} %all-gather.2.cloned.1.call-done, bf16[4096,256]{1,0:T(8,128)(2,1)} %param.16), kind=kOutput, calls=%fused_computation.12 | convolution fusion | flops 1073872896 | bytes 6553600 | tf_op jit(solution)/shard_map/dot_general | solution.py:131
  132.1 1.3 convolution_convert_fusion.1
  133.3 0.0 copy-done
  133.4 3.2 convolution_convert_fusion
  136.6 0.0 copy-start.1
  136.6 0.0 reduce-scatter.2.cloned.1.call-update
  136.6 0.0 copy-start.2
  136.6 1.0 copy-done.1
  137.6 0.8 copy.27
  138.5 5.2 %all-to-all-start = ((bf16[64,8,512]{2,0,1:T(8,128)(2,1)}), bf16[64,8,512]{2,0,1:T(8,128)(2,1)S(1)}, u32[]{:S(2)}, u32[]{:S(2)}) async-start(bf16[64,8,512]{2,0,1:T(8,128)(2,1)} %bitcast.56), calls=%async_computation | async-start | bytes 1048576 | tf_op jit(solution)/shard_map/all_to_all | solution.py:135
  143.7 0.1 fusion.37
  143.8 0.1 compare_select_fusion
  143.9 0.1 reshape.606
  144.0 0.1 compare_and_fusion
  144.1 26.3 %all-to-all-done = bf16[64,8,512]{2,0,1:T(8,128)(2,1)S(1)} async-done(((bf16[64,8,512]{2,0,1:T(8,128)(2,1)}), bf16[64,8,512]{2,0,1:T(8,128)(2,1)S(1)}, u32[]{:S(2)}, u32[]{:S(2)}) %all-to-all-start) | async-done | bytes 524320 | tf_op jit(solution)/shard_map/all_to_all | solution.py:135
  170.4 91.1 %reduce-scatter.2.cloned.1.call-done = bf16[512,512]{1,0:T(8,128)(2,1)} async-done(((bf16[512,4096]{1,0:T(8,128)(2,1)}), bf16[512,512]{1,0:T(8,128)(2,1)}) %reduce-scatter.2.cloned.1.call-update) | async-done | bytes 524304 | tf_op jit(solution)/shard_map/reduce_scatter | solution.py:153
  261.5 0.0 copy-done.2
  261.5 1.2 fusion.8
  262.7 0.0 copy-start.5
  262.7 2.0 gather_fusion
  264.7 0.1 gather.8
  264.8 0.3 select_select_fusion
  265.1 0.3 collective-permute-start
  265.4 0.0 copy-done.5
  265.4 0.6 constant_dynamic-slice_fusion
  266.7 9.1 %collective-permute-done = bf16[1,81,4,512]{3,2,1,0:T(4,128)(2,1)S(1)} collective-permute-done((bf16[1,81,4,512]{3,2,1,0:T(4,128)(2,1)S(1)}, bf16[1,81,4,512]{3,2,1,0:T(4,128)(2,1)S(1)}, u32[]{:S(2)}, u32[]{:S(2)}) %collective-permute-start) | collective-permute-done | bytes 331808 | tf_op jit(solution)/shard_map/ppermute | solution.py:15
  275.9 0.4 broadcast_select_fusion
  276.2 0.1 collective-permute-start.1
  276.3 11.8 %collective-permute-done.1 = bf16[1,81,4,512]{3,2,1,0:T(4,128)(2,1)S(1)} collective-permute-done((bf16[1,81,4,512]{3,2,1,0:T(4,128)(2,1)S(1)}, bf16[1,81,4,512]{3,2,1,0:T(4,128)(2,1)S(1)}, u32[]{:S(2)}, u32[]{:S(2)}) %collective-permute-start.1) | collective-permute-done | bytes 331808 | tf_op jit(solution)/shard_map/ppermute | solution.py:15
  288.1 0.2 broadcast_select_fusion.1
  288.3 0.1 collective-permute-start.2
  288.4 13.1 %collective-permute-done.2 = bf16[1,81,4,512]{3,2,1,0:T(4,128)(2,1)S(1)} collective-permute-done((bf16[1,81,4,512]{3,2,1,0:T(4,128)(2,1)S(1)}, bf16[1,81,4,512]{3,2,1,0:T(4,128)(2,1)S(1)}, u32[]{:S(2)}, u32[]{:S(2)}) %collective-permute-start.2) | collective-permute-done | bytes 331808 | tf_op jit(solution)/shard_map/ppermute | solution.py:15
  301.5 0.2 broadcast_select_fusion.2
  301.7 0.1 collective-permute-start.3
  301.8 10.4 %collective-permute-done.3 = bf16[1,81,4,512]{3,2,1,0:T(4,128)(2,1)S(1)} collective-permute-done((bf16[1,81,4,512]{3,2,1,0:T(4,128)(2,1)S(1)}, bf16[1,81,4,512]{3,2,1,0:T(4,128)(2,1)S(1)}, u32[]{:S(2)}, u32[]{:S(2)}) %collective-permute-start.3) | collective-permute-done | bytes 331808 | tf_op jit(solution)/shard_map/ppermute | solution.py:15
  312.3 0.2 broadcast_select_fusion.3
  312.5 0.1 collective-permute-start.4
  312.6 9.9 %collective-permute-done.4 = bf16[1,81,4,512]{3,2,1,0:T(4,128)(2,1)S(1)} collective-permute-done((bf16[1,81,4,512]{3,2,1,0:T(4,128)(2,1)S(1)}, bf16[1,81,4,512]{3,2,1,0:T(4,128)(2,1)S(1)}, u32[]{:S(2)}, u32[]{:S(2)}) %collective-permute-start.4) | collective-permute-done | bytes 331808 | tf_op jit(solution)/shard_map/ppermute | solution.py:15
  322.5 0.9 select_bitcast_fusion
  (10 shorter events, 0.1 us)
Async XLA Ops:
  6.5 126.8 %copy-start = (bf16[256,4096]{1,0:T(8,128)(2,1)S(1)}, bf16[256,4096]{1,0:T(8,128)(2,1)}, u32[]{:S(2)}) copy-start(bf16[256,4096]{1,0:T(8,128)(2,1)} %param.17) | copy-start | bytes 6291460
  6.5 113.8 %all-gather.2.cloned.1.call-start = ((), (), s32[]{:S(2)}) async-start(), calls=%async_computation.2 | async-start | bytes 4718592 | tf_op jit(solution)/shard_map/all_gather | solution.py:124
  11.4 250.0 %reduce-scatter.2.cloned.1.call-start = ((), (), s32[]{:S(2)}) async-start(), calls=%async_computation.3 | async-start | bytes 4718592 | tf_op jit(solution)/shard_map/reduce_scatter | solution.py:153
  120.4 4.4 %copy-start.3 = (bf16[512,4096]{1,0:T(8,128)(2,1)S(1)}, bf16[512,4096]{1,0:T(8,128)(2,1)}, u32[]{:S(2)}) copy-start(bf16[512,4096]{1,0:T(8,128)(2,1)} %all-gather.2.cloned.1.call-done) | copy-start | bytes 12582916
  120.4 4.7 %copy-start.4 = (bf16[4096,256]{1,0:T(8,128)(2,1)S(1)}, bf16[4096,256]{1,0:T(8,128)(2,1)}, u32[]{:S(2)}) copy-start(bf16[4096,256]{1,0:T(8,128)(2,1)} %param.15) | copy-start | bytes 6291460
  136.6 1.0 copy-start.1
  136.6 124.9 %copy-start.2 = (f32[512]{0:T(512)S(1)}, f32[512]{0:T(512)}, u32[]{:S(2)}) copy-start(f32[512]{0:T(512)} %param.18) | copy-start | bytes 6148
  138.5 31.9 %all-to-all-start = ((bf16[64,8,512]{2,0,1:T(8,128)(2,1)}), bf16[64,8,512]{2,0,1:T(8,128)(2,1)S(1)}, u32[]{:S(2)}, u32[]{:S(2)}) async-start(bf16[64,8,512]{2,0,1:T(8,128)(2,1)} %bitcast.56), calls=%async_computation | async-start | bytes 1048576 | tf_op jit(solution)/shard_map/all_to_all | solution.py:135
  262.7 2.7 copy-start.5
  265.1 10.7 %collective-permute-start = (bf16[1,81,4,512]{3,2,1,0:T(4,128)(2,1)S(1)}, bf16[1,81,4,512]{3,2,1,0:T(4,128)(2,1)S(1)}, u32[]{:S(2)}, u32[]{:S(2)}) collective-permute-start(bf16[1,81,4,512]{3,2,1,0:T(4,128)(2,1)S(1)} %select_select_fusion), channel_id=1, source_target_pairs={{0,8},{8,16},{16,24},{24,32},{32,40},{40,48},{48,56},{56,64},{64,7... | collective-permute-start | bytes 995336 | tf_op jit(solution)/shard_map/ppermute | solution.py:15
  276.2 11.9 %collective-permute-start.1 = (bf16[1,81,4,512]{3,2,1,0:T(4,128)(2,1)S(1)}, bf16[1,81,4,512]{3,2,1,0:T(4,128)(2,1)S(1)}, u32[]{:S(2)}, u32[]{:S(2)}) collective-permute-start(bf16[1,81,4,512]{3,2,1,0:T(4,128)(2,1)S(1)} %broadcast_select_fusion), channel_id=1, source_target_pairs={{0,16},{8,24},{16,32},{24,40},{32,48},{40,56},{48,64},{56,72},{64,... | collective-permute-start | bytes 995336 | tf_op jit(solution)/shard_map/ppermute | solution.py:15
  288.3 13.2 %collective-permute-start.2 = (bf16[1,81,4,512]{3,2,1,0:T(4,128)(2,1)S(1)}, bf16[1,81,4,512]{3,2,1,0:T(4,128)(2,1)S(1)}, u32[]{:S(2)}, u32[]{:S(2)}) collective-permute-start(bf16[1,81,4,512]{3,2,1,0:T(4,128)(2,1)S(1)} %broadcast_select_fusion.1), channel_id=1, source_target_pairs={{0,32},{8,40},{16,48},{24,56},{32,64},{40,72},{48,80},{56,88},{64,... | collective-permute-start | bytes 995336 | tf_op jit(solution)/shard_map/ppermute | solution.py:15
  301.7 10.6 %collective-permute-start.3 = (bf16[1,81,4,512]{3,2,1,0:T(4,128)(2,1)S(1)}, bf16[1,81,4,512]{3,2,1,0:T(4,128)(2,1)S(1)}, u32[]{:S(2)}, u32[]{:S(2)}) collective-permute-start(bf16[1,81,4,512]{3,2,1,0:T(4,128)(2,1)S(1)} %broadcast_select_fusion.2), channel_id=1, source_target_pairs={{0,64},{8,72},{16,80},{24,88},{32,96},{40,104},{48,112},{56,120},{... | collective-permute-start | bytes 995336 | tf_op jit(solution)/shard_map/ppermute | solution.py:15
  312.5 10.0 %collective-permute-start.4 = (bf16[1,81,4,512]{3,2,1,0:T(4,128)(2,1)S(1)}, bf16[1,81,4,512]{3,2,1,0:T(4,128)(2,1)S(1)}, u32[]{:S(2)}, u32[]{:S(2)}) collective-permute-start(bf16[1,81,4,512]{3,2,1,0:T(4,128)(2,1)S(1)} %broadcast_select_fusion.3), channel_id=1, source_target_pairs={{0,128},{8,136},{16,144},{24,152},{32,160},{40,168},{48,176},{56,1... | collective-permute-start | bytes 995336 | tf_op jit(solution)/shard_map/ppermute | solution.py:15
Sparse Core Ops, SparseCore 0:
  11.6 108.7 all-gather.1
  136.7 124.7 reduce-scatter.1
where the time goes:
time: 331 us; the launch traced here: 330 us
  waiting for transfers between devices  278 us (84%)
  between operations  15.8 us (5%)
  matrix products  15.2 us (5%)
  other arithmetic  10.4 us (3%)
  starting transfers between devices  5.84 us (2%)
  local copies, waits for them, and re-layouts  5.13 us (2%)
    all_gather x1, waiting for transfers between devices, body(): lax.all_gather(layer_norm(stream_rows, ln_gain, ln_bias), 'fsdp', axis=0,...  106 us
    reduce_scatter x1, waiting for transfers between devices, body(): lax.psum_scatter(partial_sum.astype(jnp.bfloat16), 'fsdp', scatter_dimens...  91.1 us
    ppermute x5, waiting for transfers between devices, shifted(): lax.ppermute(array, axis, [(i, (i + by) % count) for i in range(count)])  54.3 us
    all_to_all x1, waiting for transfers between devices, body(): lax.all_to_all(stream_rows, 'fsdp', split_axis=1, concat_axis=0, tiled=True)  26.3 us
  transfers between devices with their start and end apart: 8, of which 8 were waited for; matrix products, arithmetic and copies ran while one was open for 1% of the time, Pallas kernels for 0%

commit v1 on v0

--- a/solution.py
+++ b/solution.py
@@ -121,8 +121,14 @@
     local_heads = head_cols // HEAD
     side_row = sides[0]
     offset_row = offsets[0]
-    shard_rows = lax.all_gather(
-        layer_norm(stream_rows, ln_gain, ln_bias), "fsdp", axis=0, tiled=True
+    shard_rows = jnp.concatenate(
+        lax.all_to_all(
+            jnp.stack([layer_norm(stream_rows, ln_gain, ln_bias)] * lax.axis_size("fsdp")),
+            "fsdp",
+            0,
+            0,
+        ),
+        axis=0,
     )
     projected = jnp.concatenate(
         [

time: 331 us -> 346 us (1.045)
  starting transfers between devices: 5.84 us -> 15.6 us
    all_gather x1 -> x0, waiting for transfers between devices: 106 us -> none  [body(): lax.all_gather(layer_norm(stream_rows, ln_gain, ln_bias), 'fsdp', axis=0,...]
    all_to_all x0 -> x1, waiting for transfers between devices: none -> 76.6 us  [body(): lax.all_to_all(jnp.stack([layer_norm(stream_rows, ln_gain, ln_bias)] * la...]
    reduce_scatter x1, waiting for transfers between devices: 91.1 us -> 139 us  [body(): lax.psum_scatter(partial_sum.astype(jnp.bfloat16), 'fsdp', scatter_dimens...]
    all_to_all x1, waiting for transfers between devices: 26.3 us -> 9.86 us  [body(): lax.all_to_all(stream_rows, 'fsdp', split_axis=1, concat_axis=0, tiled=True)]
    all_to_all x0 -> x1, starting transfers between devices: none -> 11.5 us  [body(): lax.all_to_all(jnp.stack([layer_norm(stream_rows, ln_gain, ln_bias)] * la...]
where the time goes in v1:
time: 346 us
  waiting for transfers between devices  280 us (81%)
  matrix products  17.6 us (5%)
  between operations  15.8 us (5%)
  starting transfers between devices  15.6 us (5%)
  other arithmetic  9.56 us (3%)
  local copies, waits for them, and re-layouts  7.27 us (2%)
    reduce_scatter x1, waiting for transfers between devices, body(): lax.psum_scatter(partial_sum.astype(jnp.bfloat16), 'fsdp', scatter_dimens...  139 us
    all_to_all x1, waiting for transfers between devices, body(): lax.all_to_all(jnp.stack([layer_norm(stream_rows, ln_gain, ln_bias)] * la...  76.6 us
    ppermute x5, waiting for transfers between devices, shifted(): lax.ppermute(array, axis, [(i, (i + by) % count) for i in range(count)])  54.2 us
    all_to_all x1, starting transfers between devices, body(): lax.all_to_all(jnp.stack([layer_norm(stream_rows, ln_gain, ln_bias)] * la...  11.5 us
    all_to_all x1, waiting for transfers between devices, body(): lax.all_to_all(stream_rows, 'fsdp', split_axis=1, concat_axis=0, tiled=True)  9.86 us
  transfers between devices with their start and end apart: 8, of which 8 were waited for; matrix products, arithmetic and copies ran while one was open for 1% of the time, Pallas kernels for 0%

profile of v1, /device:TPU:8, one launch (start us, length us, event | category | flops | bytes accessed | tf_op | source)
XLA Modules:
  0.0 345.7 jit_solution(14563132074367603790)
XLA Ops:
  6.5 0.0 copy-start
  6.5 1.4 convert_reduce_fusion
  7.9 1.3 fusion.4
  9.3 1.3 fusion.7
  10.6 2.5 stack.6
  13.1 11.5 %all-to-all-start.1 = ((bf16[8,64,4096]{2,1,0:T(8,128)(2,1)}), bf16[8,64,4096]{2,1,0:T(8,128)(2,1)}, u32[]{:S(2)}, u32[]{:S(2)}) async-start(bf16[8,64,4096]{2,1,0:T(8,128)(2,1)} %stack.6), calls=%async_computation.1 | async-start | bytes 8388608 | tf_op jit(solution)/shard_map/all_to_all | solution.py:125
  24.6 0.0 reduce-scatter.2.cloned.1.call-start
  26.0 0.1 add_select_fusion.2
  26.1 0.2 broadcast_compare_fusion
  26.4 1.0 fusion.17
  27.4 76.6 %all-to-all-done.1 = bf16[8,64,4096]{2,1,0:T(8,128)(2,1)} async-done(((bf16[8,64,4096]{2,1,0:T(8,128)(2,1)}), bf16[8,64,4096]{2,1,0:T(8,128)(2,1)}, u32[]{:S(2)}, u32[]{:S(2)}) %all-to-all-start.1) | async-done | bytes 4194336 | tf_op jit(solution)/shard_map/all_to_all | solution.py:125
  104.0 0.0 copy-start.3
  104.0 5.0 %convolution_convert_fusion.2 = bf16[512,256]{0,1:T(8,128)(2,1)} fusion(bf16[512,4096]{1,0:T(8,128)(2,1)} %bitcast.11, bf16[4096,256]{1,0:T(8,128)(2,1)} %param.16), kind=kOutput, calls=%fused_computation.12 | convolution fusion | flops 1073872896 | bytes 6553600 | tf_op jit(solution)/shard_map/dot_general | solution.py:137
  109.0 0.0 copy-done.3
  109.0 0.0 copy-start.4
  109.0 3.6 %fusion.47 = f32[512,256]{0,1:T(8,128)S(1)} fusion(bf16[512,4096]{1,0:T(8,128)(2,1)} %bitcast.11, bf16[4096,256]{1,0:T(8,128)(2,1)S(1)} %copy-done.3), kind=kOutput, calls=%fused_computation.99 | convolution fusion | flops 1073741824 | bytes 6815744 | tf_op jit(solution)/shard_map/dot_general | solution.py:135
  112.7 0.0 copy-done.4
  112.7 3.5 %fusion.48 = f32[512,256]{0,1:T(8,128)S(1)} fusion(bf16[512,4096]{1,0:T(8,128)(2,1)} %bitcast.11, bf16[4096,256]{1,0:T(8,128)(2,1)S(1)} %copy-done.4), kind=kOutput, calls=%fused_computation.100 | convolution fusion | flops 1073741824 | bytes 6815744 | tf_op jit(solution)/shard_map/dot_general | solution.py:136
  116.3 0.1 pad_maximum_fusion
  116.4 0.3 fusion.13
  116.7 0.0 copy-start.6
  116.7 1.0 fusion.46
  117.7 0.0 copy-done.6
  117.7 1.3 convolution_convert_fusion.1
  119.0 0.0 copy-done
  119.0 3.2 convolution_convert_fusion
  122.2 0.0 copy-start.1
  122.2 0.0 reduce-scatter.2.cloned.1.call-update
  122.2 0.0 copy-start.2
  122.3 1.0 copy-done.1
  123.3 0.8 copy.27
  124.1 3.6 %all-to-all-start = ((bf16[64,8,512]{2,0,1:T(8,128)(2,1)}), bf16[64,8,512]{2,0,1:T(8,128)(2,1)S(1)}, u32[]{:S(2)}, u32[]{:S(2)}) async-start(bf16[64,8,512]{2,0,1:T(8,128)(2,1)} %bitcast.57), calls=%async_computation | async-start | bytes 1048576 | tf_op jit(solution)/shard_map/all_to_all | solution.py:141
  127.8 0.1 fusion.37
  127.9 0.1 compare_select_fusion
  128.0 0.1 reshape.612
  128.2 0.1 compare_and_fusion
  128.3 9.9 %all-to-all-done = bf16[64,8,512]{2,0,1:T(8,128)(2,1)S(1)} async-done(((bf16[64,8,512]{2,0,1:T(8,128)(2,1)}), bf16[64,8,512]{2,0,1:T(8,128)(2,1)S(1)}, u32[]{:S(2)}, u32[]{:S(2)}) %all-to-all-start) | async-done | bytes 524320 | tf_op jit(solution)/shard_map/all_to_all | solution.py:141
  138.1 139.1 %reduce-scatter.2.cloned.1.call-done = bf16[512,512]{1,0:T(8,128)(2,1)} async-done(((bf16[512,4096]{1,0:T(8,128)(2,1)}), bf16[512,512]{1,0:T(8,128)(2,1)}) %reduce-scatter.2.cloned.1.call-update) | async-done | bytes 524304 | tf_op jit(solution)/shard_map/reduce_scatter | solution.py:159
  277.3 0.0 copy-done.2
  277.3 1.2 fusion.8
  278.5 0.0 copy-start.5
  278.5 2.0 gather_fusion
  280.5 0.1 gather.8
  280.6 0.3 select_select_fusion
  280.9 0.1 collective-permute-start
  281.0 0.0 copy-done.5
  281.0 0.6 constant_dynamic-slice_fusion
  282.3 9.1 %collective-permute-done = bf16[1,81,4,512]{3,2,1,0:T(4,128)(2,1)S(1)} collective-permute-done((bf16[1,81,4,512]{3,2,1,0:T(4,128)(2,1)S(1)}, bf16[1,81,4,512]{3,2,1,0:T(4,128)(2,1)S(1)}, u32[]{:S(2)}, u32[]{:S(2)}) %collective-permute-start) | collective-permute-done | bytes 331808 | tf_op jit(solution)/shard_map/ppermute | solution.py:15
  291.5 0.4 broadcast_select_fusion
  291.8 0.1 collective-permute-start.1
  292.0 11.9 %collective-permute-done.1 = bf16[1,81,4,512]{3,2,1,0:T(4,128)(2,1)S(1)} collective-permute-done((bf16[1,81,4,512]{3,2,1,0:T(4,128)(2,1)S(1)}, bf16[1,81,4,512]{3,2,1,0:T(4,128)(2,1)S(1)}, u32[]{:S(2)}, u32[]{:S(2)}) %collective-permute-start.1) | collective-permute-done | bytes 331808 | tf_op jit(solution)/shard_map/ppermute | solution.py:15
  303.8 0.2 broadcast_select_fusion.1
  304.0 0.1 collective-permute-start.2
  304.1 13.0 %collective-permute-done.2 = bf16[1,81,4,512]{3,2,1,0:T(4,128)(2,1)S(1)} collective-permute-done((bf16[1,81,4,512]{3,2,1,0:T(4,128)(2,1)S(1)}, bf16[1,81,4,512]{3,2,1,0:T(4,128)(2,1)S(1)}, u32[]{:S(2)}, u32[]{:S(2)}) %collective-permute-start.2) | collective-permute-done | bytes 331808 | tf_op jit(solution)/shard_map/ppermute | solution.py:15
  317.2 0.2 broadcast_select_fusion.2
  317.3 0.1 collective-permute-start.3
  317.5 10.4 %collective-permute-done.3 = bf16[1,81,4,512]{3,2,1,0:T(4,128)(2,1)S(1)} collective-permute-done((bf16[1,81,4,512]{3,2,1,0:T(4,128)(2,1)S(1)}, bf16[1,81,4,512]{3,2,1,0:T(4,128)(2,1)S(1)}, u32[]{:S(2)}, u32[]{:S(2)}) %collective-permute-start.3) | collective-permute-done | bytes 331808 | tf_op jit(solution)/shard_map/ppermute | solution.py:15
  327.8 0.2 broadcast_select_fusion.3
  328.0 0.1 collective-permute-start.4
  328.1 9.8 %collective-permute-done.4 = bf16[1,81,4,512]{3,2,1,0:T(4,128)(2,1)S(1)} collective-permute-done((bf16[1,81,4,512]{3,2,1,0:T(4,128)(2,1)S(1)}, bf16[1,81,4,512]{3,2,1,0:T(4,128)(2,1)S(1)}, u32[]{:S(2)}, u32[]{:S(2)}) %collective-permute-start.4) | collective-permute-done | bytes 331808 | tf_op jit(solution)/shard_map/ppermute | solution.py:15
  337.9 0.9 select_bitcast_fusion
  (10 shorter events, 0.1 us)
Async XLA Ops:
  6.5 112.4 %copy-start = (bf16[256,4096]{1,0:T(8,128)(2,1)S(1)}, bf16[256,4096]{1,0:T(8,128)(2,1)}, u32[]{:S(2)}) copy-start(bf16[256,4096]{1,0:T(8,128)(2,1)} %param.17) | copy-start | bytes 6291460
  13.1 90.9 %all-to-all-start.1 = ((bf16[8,64,4096]{2,1,0:T(8,128)(2,1)}), bf16[8,64,4096]{2,1,0:T(8,128)(2,1)}, u32[]{:S(2)}, u32[]{:S(2)}) async-start(bf16[8,64,4096]{2,1,0:T(8,128)(2,1)} %stack.6), calls=%async_computation.1 | async-start | bytes 8388608 | tf_op jit(solution)/shard_map/all_to_all | solution.py:125
  24.6 252.6 %reduce-scatter.2.cloned.1.call-start = ((), (), s32[]{:S(2)}) async-start(), calls=%async_computation.3 | async-start | bytes 4718592 | tf_op jit(solution)/shard_map/reduce_scatter | solution.py:159
  104.0 5.0 %copy-start.3 = (bf16[4096,256]{1,0:T(8,128)(2,1)S(1)}, bf16[4096,256]{1,0:T(8,128)(2,1)}, u32[]{:S(2)}) copy-start(bf16[4096,256]{1,0:T(8,128)(2,1)} %param.14) | copy-start | bytes 6291460
  109.0 3.7 %copy-start.4 = (bf16[4096,256]{1,0:T(8,128)(2,1)S(1)}, bf16[4096,256]{1,0:T(8,128)(2,1)}, u32[]{:S(2)}) copy-start(bf16[4096,256]{1,0:T(8,128)(2,1)} %param.15) | copy-start | bytes 6291460
  116.7 1.0 copy-start.6
  122.2 1.0 copy-start.1
  122.2 155.0 %copy-start.2 = (f32[512]{0:T(512)S(1)}, f32[512]{0:T(512)}, u32[]{:S(2)}) copy-start(f32[512]{0:T(512)} %param.18) | copy-start | bytes 6148
  124.1 14.0 %all-to-all-start = ((bf16[64,8,512]{2,0,1:T(8,128)(2,1)}), bf16[64,8,512]{2,0,1:T(8,128)(2,1)S(1)}, u32[]{:S(2)}, u32[]{:S(2)}) async-start(bf16[64,8,512]{2,0,1:T(8,128)(2,1)} %bitcast.57), calls=%async_computation | async-start | bytes 1048576 | tf_op jit(solution)/shard_map/all_to_all | solution.py:141
  278.5 2.6 copy-start.5
  280.9 10.5 %collective-permute-start = (bf16[1,81,4,512]{3,2,1,0:T(4,128)(2,1)S(1)}, bf16[1,81,4,512]{3,2,1,0:T(4,128)(2,1)S(1)}, u32[]{:S(2)}, u32[]{:S(2)}) collective-permute-start(bf16[1,81,4,512]{3,2,1,0:T(4,128)(2,1)S(1)} %select_select_fusion), channel_id=1, source_target_pairs={{0,8},{8,16},{16,24},{24,32},{32,40},{40,48},{48,56},{56,64},{64,7... | collective-permute-start | bytes 995336 | tf_op jit(solution)/shard_map/ppermute | solution.py:15
  291.8 12.0 %collective-permute-start.1 = (bf16[1,81,4,512]{3,2,1,0:T(4,128)(2,1)S(1)}, bf16[1,81,4,512]{3,2,1,0:T(4,128)(2,1)S(1)}, u32[]{:S(2)}, u32[]{:S(2)}) collective-permute-start(bf16[1,81,4,512]{3,2,1,0:T(4,128)(2,1)S(1)} %broadcast_select_fusion), channel_id=1, source_target_pairs={{0,16},{8,24},{16,32},{24,40},{32,48},{40,56},{48,64},{56,72},{64,... | collective-permute-start | bytes 995336 | tf_op jit(solution)/shard_map/ppermute | solution.py:15
  304.0 13.1 %collective-permute-start.2 = (bf16[1,81,4,512]{3,2,1,0:T(4,128)(2,1)S(1)}, bf16[1,81,4,512]{3,2,1,0:T(4,128)(2,1)S(1)}, u32[]{:S(2)}, u32[]{:S(2)}) collective-permute-start(bf16[1,81,4,512]{3,2,1,0:T(4,128)(2,1)S(1)} %broadcast_select_fusion.1), channel_id=1, source_target_pairs={{0,32},{8,40},{16,48},{24,56},{32,64},{40,72},{48,80},{56,88},{64,... | collective-permute-start | bytes 995336 | tf_op jit(solution)/shard_map/ppermute | solution.py:15
  317.3 10.5 %collective-permute-start.3 = (bf16[1,81,4,512]{3,2,1,0:T(4,128)(2,1)S(1)}, bf16[1,81,4,512]{3,2,1,0:T(4,128)(2,1)S(1)}, u32[]{:S(2)}, u32[]{:S(2)}) collective-permute-start(bf16[1,81,4,512]{3,2,1,0:T(4,128)(2,1)S(1)} %broadcast_select_fusion.2), channel_id=1, source_target_pairs={{0,64},{8,72},{16,80},{24,88},{32,96},{40,104},{48,112},{56,120},{... | collective-permute-start | bytes 995336 | tf_op jit(solution)/shard_map/ppermute | solution.py:15
  328.0 9.9 %collective-permute-start.4 = (bf16[1,81,4,512]{3,2,1,0:T(4,128)(2,1)S(1)}, bf16[1,81,4,512]{3,2,1,0:T(4,128)(2,1)S(1)}, u32[]{:S(2)}, u32[]{:S(2)}) collective-permute-start(bf16[1,81,4,512]{3,2,1,0:T(4,128)(2,1)S(1)} %broadcast_select_fusion.3), channel_id=1, source_target_pairs={{0,128},{8,136},{16,144},{24,152},{32,160},{40,168},{48,176},{56,1... | collective-permute-start | bytes 995336 | tf_op jit(solution)/shard_map/ppermute | solution.py:15
Sparse Core Ops, SparseCore 0:
  122.4 154.8 reduce-scatter.1
